TPU v7x, 512 devices: a whole 4x4x16 slice. The times are simulated.
512 devices in a mesh: tile: 64 (over z, x), image: 2 (over y_hi), tensor: 4 (over y_lo, core).
Axes of the slice: x: 4, y: 4 (y_hi: 2, y_lo: 2; y = y_hi * 2 + y_lo), z: 16, core: 2. Of those that a mesh axis runs over, the one named last changes fastest.
Arguments:
- latent: bfloat16 [2, 256, 640, 128], P('image', 'tile', 'tensor'), may hold values from -8 to 8
- tile_slot: int32 [2, 64], replicated, may hold values from 0 to 63, each once within a row
- tile_count: int32 [2], replicated, may hold values from 16 to 64, as said below
- merge_num: int32 [1], replicated, may hold values from 3 to 13
- conv_ema: bfloat16 [3, 3, 4, 2, 80, 640], P(None, None, 'tensor', 'image'), may hold values from -0.078125 to 0.078125
- conv_adjusted: bfloat16 [3, 3, 4, 2, 80, 640], P(None, None, 'tensor', 'image'), may hold values from -0.078125 to 0.078125
- query_ema: bfloat16 [640, 512], P('image', 'tensor'), may hold values from -4 to 4
- query_adjusted: bfloat16 [640, 512], P('image', 'tensor'), may hold values from -4 to 4
- kv_ema: bfloat16 [640, 2, 512], P('image', None, 'tensor'), may hold values from -4 to 4
- kv_adjusted: bfloat16 [640, 2, 512], P('image', None, 'tensor'), may hold values from -4 to 4
- out_ema: bfloat16 [640, 512], P('tensor', 'image'), may hold values from -0.25 to 0.25
- out_adjusted: bfloat16 [640, 512], P('tensor', 'image'), may hold values from -0.25 to 0.25
- norm_gain: bfloat16 [640], replicated, may hold values from 0.099609375 to 1.8984375
Outputs:
- denoised: bfloat16 [2, 256, 640, 128], P('image', 'tile', 'tensor')
Inputs may be any that keep to these rules, and one draw needn't show every extreme that they name: `tile_count`: the number of live tiles of each image; exactly one image has all 64 live, the others fewer. `tile_slot`: each row is a permutation of the tiles' vertical positions.
All inputs are finite; a program needn't handle non-finite values.
Results may differ from a plain program's by a relative error of at most 0.007.
The roundings to bfloat16 on the way count: a program that leaves them out, or rounds other values in their place, can miss the bound.
Values may be sent and summed in bfloat16 or wider, within the bound.
No kernel may reach another device: no remote copies, remote signals or barrier semaphores. Data moves between devices by JAX's collectives and lax.ppermute only.
A program may use at most 64 MiB of HBM per device.

v0:
```python
import jax
import jax.numpy as jnp
from jax import lax
from jax.sharding import PartitionSpec as P

HD = 64
POOL = 4


def blend(ema_part, adjusted_part, blend_ratio):
    base = ema_part.astype(jnp.float32)
    return (base + blend_ratio * (adjusted_part.astype(jnp.float32) - base)).astype(jnp.bfloat16)


def convolve(field, kernel, row_padding):
    return lax.conv_general_dilated(
        field[None],
        kernel,
        (1, 1),
        (row_padding, (1, 1)),
        dimension_numbers=("NHCW", "HWOI", "NHCW"),
        preferred_element_type=jnp.float32,
    )[0]


def slot_lookup(tile_ids, slot_row):
    tile_total = slot_row.shape[0]
    matches = tile_ids[:, None] == jnp.arange(tile_total, dtype=jnp.int32)[None, :]
    return jnp.sum(jnp.where(matches, slot_row[None, :], 0), axis=1)


def on_device(
    latent,
    tile_slot,
    tile_count,
    merge_num,
    conv_ema,
    conv_adjusted,
    query_ema,
    query_adjusted,
    kv_ema,
    kv_adjusted,
    out_ema,
    out_adjusted,
    norm_gain,
):
    image_index = lax.axis_index("image")
    tile_index = lax.axis_index("tile")
    slot_row = lax.dynamic_index_in_dim(tile_slot, image_index, 0, keepdims=False)
    live_count = lax.dynamic_index_in_dim(tile_count, image_index, 0, keepdims=False)
    my_slot = lax.dynamic_index_in_dim(slot_row, tile_index, 0, keepdims=False)
    live_flag = (my_slot < live_count).astype(jnp.float32)
    blend_ratio = merge_num[0].astype(jnp.float32) / 16.0
    gathered = (
        lax.all_gather(conv_ema, "image", axis=3, tiled=True),
        lax.all_gather(conv_adjusted, "image", axis=3, tiled=True),
        lax.all_gather(query_ema, "image", axis=0, tiled=True),
        lax.all_gather(query_adjusted, "image", axis=0, tiled=True),
        lax.all_gather(kv_ema, "image", axis=0, tiled=True),
        lax.all_gather(kv_adjusted, "image", axis=0, tiled=True),
        lax.all_gather(out_ema, "image", axis=1, tiled=True),
        lax.all_gather(out_adjusted, "image", axis=1, tiled=True),
    )
    conv_w = blend(gathered[0], gathered[1], blend_ratio)
    query_w = blend(gathered[2], gathered[3], blend_ratio)
    kv_w = blend(gathered[4], gathered[5], blend_ratio)
    out_w = blend(gathered[6], gathered[7], blend_ratio)
    conv_w = conv_w.reshape(3, 3, -1, conv_w.shape[-1])
    feats = latent[0]
    tile_rows, chan_shard, tile_cols = feats.shape
    activated = jax.nn.silu(feats.astype(jnp.float32)).astype(jnp.bfloat16)
    block_full = lax.all_gather(activated, "tensor", axis=1, tiled=True)
    rim_rows = jnp.stack([activated[0], activated[-1]])[None]
    shard_piece = lax.all_gather(rim_rows, "tile", axis=0, tiled=True)
    source = jnp.arange(shard_piece.shape[0], dtype=jnp.int32)
    source_slot = slot_lookup(source, slot_row)
    upper_w = (source_slot == my_slot - 1).astype(jnp.float32)
    lower_w = jnp.logical_and(source_slot == my_slot + 1, source_slot < live_count).astype(
        jnp.float32
    )
    piece_f = shard_piece.astype(jnp.float32)
    upper = jnp.einsum("n,ncw->cw", upper_w, piece_f[:, 1])
    lower = jnp.einsum("n,ncw->cw", lower_w, piece_f[:, 0])
    halo_rows = jnp.stack([upper, lower]).astype(jnp.bfloat16)
    halo_full = lax.all_gather(halo_rows, "tensor", axis=1, tiled=True)
    padded = jnp.concatenate([halo_full[0:1], block_full, halo_full[1:2]], axis=0)
    conv_out = convolve(padded, conv_w, (0, 0))
    section = (feats.astype(jnp.float32) + conv_out).astype(jnp.bfloat16)
    section_full = lax.all_gather(section, "tensor", axis=1, tiled=True)
    channels = section_full.shape[1]
    cells = tile_rows * tile_cols
    section_f = section_full.astype(jnp.float32)
    rows_f = jnp.transpose(section_f, (0, 2, 1)).reshape(cells, channels)
    root_mean = jnp.sqrt(jnp.mean(rows_f * rows_f, axis=-1) + 1e-06)
    normed = (rows_f * norm_gain.astype(jnp.float32) / root_mean[:, None]).astype(jnp.bfloat16)
    queries = (jnp.dot(normed, query_w, preferred_element_type=jnp.float32) * HD ** (-0.5)).astype(
        jnp.bfloat16
    )
    att_shard = queries.shape[1]
    head_count = att_shard // HD
    pooled = section_f.reshape(tile_rows // POOL, POOL, channels, tile_cols // POOL, POOL).mean(
        axis=(1, 4)
    )
    tok_count = pooled.shape[0] * pooled.shape[2]
    pooled = jnp.transpose(pooled, (0, 2, 1)).astype(jnp.bfloat16).reshape(tok_count, channels)
    kv_flat = kv_w.reshape(channels, 2 * att_shard)
    block_rows = min(512, cells)
    blocks = cells // block_rows
    query_blocks = queries.reshape(blocks, block_rows, head_count, HD)
    start_state = (
        jnp.full((blocks, block_rows, head_count), -1e30, jnp.float32),
        jnp.zeros((blocks, block_rows, head_count), jnp.float32),
        jnp.zeros((blocks, block_rows, head_count, HD), jnp.float32),
    )
    kv_rows = jnp.dot(
        lax.all_gather(pooled, "tile", axis=0, tiled=True),
        kv_flat,
        preferred_element_type=jnp.float32,
    ).astype(jnp.bfloat16)
    key_rows = kv_rows[:, :att_shard]
    key_total = key_rows.shape[0]
    key_tile = jnp.arange(key_total, dtype=jnp.int32) // tok_count
    key_live = slot_lookup(key_tile, slot_row) < live_count
    key_livef = key_live.astype(jnp.float32)
    key_heads = key_rows.reshape(key_total, head_count, HD)
    value_heads = kv_rows[:, att_shard:].reshape(key_total, head_count, HD)

    def per_block(inputs):
        query_part, max_part, total_part, accum_part = inputs
        max_list, total_list, accum_list = ([], [], [])
        for head_index in range(head_count):
            scores = lax.dot_general(
                query_part[:, head_index],
                key_heads[:, head_index],
                (((1,), (1,)), ((), ())),
                preferred_element_type=jnp.float32,
            )
            scores = jnp.where(key_live[None, :], scores, -1e30)
            max_new = jnp.maximum(max_part[:, head_index], jnp.max(scores, axis=1))
            expd = jnp.exp(scores - max_new[:, None]) * key_livef[None, :]
            shrink = jnp.exp(max_part[:, head_index] - max_new)
            max_list.append(max_new)
            total_list.append(total_part[:, head_index] * shrink + jnp.sum(expd, axis=1))
            accum_list.append(
                accum_part[:, head_index] * shrink[:, None]
                + jnp.dot(
                    expd.astype(jnp.bfloat16),
                    value_heads[:, head_index],
                    preferred_element_type=jnp.float32,
                )
            )
        return (
            jnp.stack(max_list, axis=1),
            jnp.stack(total_list, axis=1),
            jnp.stack(accum_list, axis=1),
        )

    final_state = lax.map(per_block, (query_blocks, start_state[0], start_state[1], start_state[2]))
    attended = (
        (final_state[2] / final_state[1][..., None]).astype(jnp.bfloat16).reshape(cells, att_shard)
    )
    shard_piece = jax.tree.map(
        lambda part: lax.all_gather(part, "tensor", axis=1, tiled=True), attended
    )
    weight_cols = lax.slice_in_dim(out_w, 0, shard_piece.shape[1], axis=1)
    projected = jnp.zeros((chan_shard, cells), jnp.float32) + lax.dot_general(
        weight_cols, shard_piece, (((1,), (1,)), ((), ())), preferred_element_type=jnp.float32
    )
    projected = jnp.transpose(projected.reshape(chan_shard, tile_rows, tile_cols), (1, 0, 2))
    final = (section.astype(jnp.float32) + projected) * live_flag
    return final.astype(jnp.bfloat16).reshape(1, tile_rows, chan_shard, tile_cols)


def solution(mesh):
    placed = (
        P("image", "tile", "tensor", None),
        P(),
        P(),
        P(),
        P(None, None, "tensor", "image", None, None),
        P(None, None, "tensor", "image", None, None),
        P("image", "tensor"),
        P("image", "tensor"),
        P("image", None, "tensor"),
        P("image", None, "tensor"),
        P("tensor", "image"),
        P("tensor", "image"),
        P(),
    )
    return jax.shard_map(
        on_device,
        mesh=mesh,
        in_specs=placed,
        out_specs=P("image", "tile", "tensor", None),
        check_vma=False,
    )
```

profile of v0, /device:TPU:1, one launch (start us, length us, event | category | flops | bytes accessed | tf_op | source)
XLA Modules:
  0.0 443.0 jit_solution(12450239543727953347)
XLA Ops:
  6.5 0.7 all-gather.7.cloned.1.call-update
  7.3 0.0 all-gather.9.cloned.1.call-start
  7.3 0.7 all-gather.9.cloned.1.call-update
  8.0 0.0 all-gather.11.cloned.1.call-start
  8.1 1.0 fusion.54
  9.1 0.6 pad_maximum_fusion.1
  9.7 0.0 all-gather.11.cloned.1.call-update
  9.8 0.0 all-gather.13.cloned.1.call-start
  9.8 0.1 copy.107
  9.9 0.6 dynamic_slice.24
  11.0 0.6 dynamic_slice.25
  12.9 0.1 select_reduce_fusion.3
  13.0 13.6 %all_gather.44 = bf16[4,640,128]{2,0,1:T(4,128)(2,1)S(1)} all-gather(bf16[4,160,128]{2,0,1:T(4,128)(2,1)S(1)} %copy.107), channel_id=1, replica_groups=mesh['tile'=64,'image'=2,'tensor'=4] {'tensor'}, dimensions={1}, use_global_device_ids=true | all-gather | bytes 819200 | tf_op jit(solution)/shard_map/all_gather | solution.py:72
  26.6 30.2 %all-gather.7.cloned.1.call-done = bf16[3,3,1,2,80,640]{5,4,3,2,1,0:T(8,128)(2,1)} async-done(((bf16[3,3,1,1,80,640]{5,4,3,2,1,0:T(8,128)(2,1)}), bf16[3,3,1,2,80,640]{5,4,3,2,1,0:T(8,128)(2,1)}) %all-gather.7.cloned.1.call-update) | async-done | bytes 1843216 | tf_op jit(solution)/shard_map/all_gather | solution.py:55
  56.8 43.6 %all-gather.9.cloned.1.call-done = bf16[3,3,1,2,80,640]{5,4,3,2,1,0:T(8,128)(2,1)} async-done(((bf16[3,3,1,1,80,640]{5,4,3,2,1,0:T(8,128)(2,1)}), bf16[3,3,1,2,80,640]{5,4,3,2,1,0:T(8,128)(2,1)}) %all-gather.9.cloned.1.call-update) | async-done | bytes 1843216 | tf_op jit(solution)/shard_map/all_gather | solution.py:56
  100.4 4.0 fusion.1
  104.4 139.5 %all-gather.11.cloned.1.call-done = bf16[128,160,128]{2,1,0:T(8,128)(2,1)} async-done(((bf16[2,160,128]{2,1,0:T(8,128)(2,1)}), bf16[128,160,128]{2,1,0:T(8,128)(2,1)}) %all-gather.11.cloned.1.call-update) | async-done | bytes 5242896 | tf_op jit(solution)/shard_map/all_gather | solution.py:74
  243.9 2.9 slice_bitcast_fusion.1
  246.8 0.8 fusion.10
  247.6 1.4 fusion.8
  249.1 15.5 %all_gather.43 = bf16[2,640,128]{2,1,0:T(8,128)(2,1)S(1)} all-gather(bf16[2,160,128]{2,1,0:T(8,128)(2,1)S(1)} %pad_maximum_fusion.2), channel_id=1, replica_groups=mesh['tile'=64,'image'=2,'tensor'=4] {'tensor'}, dimensions={1}, use_global_device_ids=true | all-gather | bytes 409600 | tf_op jit(solution)/shard_map/all_gather | solution.py:85
  264.6 0.3 copy.108
  264.9 0.3 copy.109
  265.1 1.1 maximum_bitcast_fusion
  266.3 1.2 copy.129
  267.5 0.3 pad.clone
  267.7 0.4 reshape.172
  268.1 0.1 copy.112
  268.3 0.1 copy-done.11
  268.4 1.2 copy-done
  269.6 1.8 convolution_select_fusion
  271.5 0.2 copy.113
  271.8 0.2 copy.128
  272.0 0.4 copy-done.1
  272.5 0.1 copy.115
  272.6 8.1 %all_gather.49 = bf16[4,640,128]{2,0,1:T(4,128)(2,1)S(1)} all-gather(bf16[4,160,128]{2,0,1:T(4,128)(2,1)S(1)} %copy.115), channel_id=1, replica_groups=mesh['tile'=64,'image'=2,'tensor'=4] {'tensor'}, dimensions={1}, use_global_device_ids=true | all-gather | bytes 819200 | tf_op jit(solution)/shard_map/all_gather | solution.py:89
  280.7 0.9 copy.116
  281.6 0.1 convert_reduce_fusion
  281.7 0.1 reduce_sum.71
  281.8 0.2 reduce_sum.72
  282.0 0.6 fusion.69
  283.9 6.1 %all_gather.50 = bf16[640,128]{1,0:T(8,128)(2,1)S(1)} all-gather(bf16[320,128]{1,0:T(8,128)(2,1)S(1)} %copy-done.4), channel_id=1, replica_groups=mesh['tile'=64,'image'=2,'tensor'=4] {'image'}, dimensions={0}, use_global_device_ids=true | all-gather | bytes 245760 | tf_op jit(solution)/shard_map/all_gather | solution.py:57
  289.9 5.5 %all_gather.51 = bf16[640,128]{1,0:T(8,128)(2,1)S(1)} all-gather(bf16[320,128]{1,0:T(8,128)(2,1)S(1)} %copy-done.5), channel_id=1, replica_groups=mesh['tile'=64,'image'=2,'tensor'=4] {'image'}, dimensions={0}, use_global_device_ids=true | all-gather | bytes 245760 | tf_op jit(solution)/shard_map/all_gather | solution.py:58
  295.4 5.5 %all_gather.47 = bf16[160,512]{1,0:T(8,128)(2,1)S(1)} all-gather(bf16[160,256]{1,0:T(8,128)(2,1)S(1)} %copy-done.6), channel_id=1, replica_groups=mesh['tile'=64,'image'=2,'tensor'=4] {'image'}, dimensions={1}, use_global_device_ids=true | all-gather | bytes 245760 | tf_op jit(solution)/shard_map/all_gather | solution.py:61
  300.9 5.5 %all_gather.48 = bf16[160,512]{1,0:T(8,128)(2,1)S(1)} all-gather(bf16[160,256]{1,0:T(8,128)(2,1)S(1)} %copy-done.7), channel_id=1, replica_groups=mesh['tile'=64,'image'=2,'tensor'=4] {'image'}, dimensions={1}, use_global_device_ids=true | all-gather | bytes 245760 | tf_op jit(solution)/shard_map/all_gather | solution.py:62
  306.3 6.4 %all_gather.53 = bf16[640,2,128]{2,1,0:T(2,128)(2,1)S(1)} all-gather(bf16[320,2,128]{2,1,0:T(2,128)(2,1)S(1)} %copy-done.2), channel_id=1, replica_groups=mesh['tile'=64,'image'=2,'tensor'=4] {'image'}, dimensions={0}, use_global_device_ids=true | all-gather | bytes 491520 | tf_op jit(solution)/shard_map/all_gather | solution.py:59
  312.7 6.9 %all_gather.54 = bf16[640,2,128]{2,1,0:T(2,128)(2,1)S(1)} all-gather(bf16[320,2,128]{2,1,0:T(2,128)(2,1)S(1)} %copy-done.3), channel_id=1, replica_groups=mesh['tile'=64,'image'=2,'tensor'=4] {'image'}, dimensions={0}, use_global_device_ids=true | all-gather | bytes 491520 | tf_op jit(solution)/shard_map/all_gather | solution.py:60
  319.6 0.2 select_reduce_fusion.2
  319.8 0.6 fusion.89
  320.4 0.5 fusion.45
  320.9 0.2 fusion.24
  321.2 0.2 fusion.23
  321.4 0.4 fusion.31
  321.7 88.4 %all-gather.13.cloned.1.call-done = bf16[1,2048,640]{2,1,0:T(8,128)(2,1)} async-done(((bf16[1,32,640]{2,1,0:T(8,128)(2,1)}), bf16[1,2048,640]{2,1,0:T(8,128)(2,1)}) %all-gather.13.cloned.1.call-update) | async-done | bytes 2621456 | tf_op jit(solution)/shard_map/all_gather | solution.py:116
  410.2 2.8 fusion.12
  412.9 0.1 fusion.90
  413.0 0.7 fusion.61
  413.7 1.1 select_reduce_fusion.1
  414.8 2.1 fusion.2
  417.0 1.0 fusion.35
  418.1 1.0 fusion.41
  419.2 16.3 %all_gather.55 = bf16[512,512]{0,1:T(8,128)(2,1)S(1)} all-gather(bf16[512,128]{0,1:T(8,128)(2,1)S(1)} %fusion.63), channel_id=1, replica_groups=mesh['tile'=64,'image'=2,'tensor'=4] {'tensor'}, dimensions={1}, use_global_device_ids=true | all-gather | bytes 655360 | tf_op jit(solution)/shard_map/all_gather | solution.py:163
  435.5 0.3 convolution_bitcast_fusion
  435.7 0.7 fusion.64
  (41 shorter events, 0.3 us)
Async XLA Ops:
  6.5 3.4 copy-start.9
  6.5 4.5 %copy-start.10 = (s32[2]{0:T(128)S(1)}, s32[2]{0:T(128)}, u32[]{:S(2)}) copy-start(s32[2]{0:T(128)} %param.15) | copy-start | bytes 28
  6.5 50.2 %all-gather.7.cloned.1.call-start = ((), (), s32[]{:S(2)}) async-start(), calls=%async_computation | async-start | bytes 2764800 | tf_op jit(solution)/shard_map/all_gather | solution.py:55
  7.3 93.1 %all-gather.9.cloned.1.call-start = ((), (), s32[]{:S(2)}) async-start(), calls=%async_computation.1 | async-start | bytes 2764800 | tf_op jit(solution)/shard_map/all_gather | solution.py:56
  8.0 235.9 %all-gather.11.cloned.1.call-start = ((), (), s32[]{:S(2)}) async-start(), calls=%async_computation.2 | async-start | bytes 5324800 | tf_op jit(solution)/shard_map/all_gather | solution.py:74
  9.8 400.4 %all-gather.13.cloned.1.call-start = ((), (), s32[]{:S(2)}) async-start(), calls=%async_computation.3 | async-start | bytes 2662400 | tf_op jit(solution)/shard_map/all_gather | solution.py:116
  267.7 0.7 copy-start.11
  268.1 1.5 copy-start
  271.5 0.9 copy-start.1
  272.4 11.4 %copy-start.8 = (bf16[640]{0:T(1024)(128)(2,1)S(1)}, bf16[640]{0:T(1024)(128)(2,1)}, u32[]{:S(2)}) copy-start(bf16[640]{0:T(1024)(128)(2,1)} %param.25) | copy-start | bytes 3844
  272.4 11.4 %copy-start.4 = (bf16[320,128]{1,0:T(8,128)(2,1)S(1)}, bf16[320,128]{1,0:T(8,128)(2,1)}, u32[]{:S(2)}) copy-start(bf16[320,128]{1,0:T(8,128)(2,1)} %param.19) | copy-start | bytes 245764
  272.5 17.5 %copy-start.5 = (bf16[320,128]{1,0:T(8,128)(2,1)S(1)}, bf16[320,128]{1,0:T(8,128)(2,1)}, u32[]{:S(2)}) copy-start(bf16[320,128]{1,0:T(8,128)(2,1)} %param.20) | copy-start | bytes 245764
  272.5 22.9 %copy-start.6 = (bf16[160,256]{1,0:T(8,128)(2,1)S(1)}, bf16[160,256]{1,0:T(8,128)(2,1)}, u32[]{:S(2)}) copy-start(bf16[160,256]{1,0:T(8,128)(2,1)} %param.23) | copy-start | bytes 245764
  272.6 28.3 %copy-start.7 = (bf16[160,256]{1,0:T(8,128)(2,1)S(1)}, bf16[160,256]{1,0:T(8,128)(2,1)}, u32[]{:S(2)}) copy-start(bf16[160,256]{1,0:T(8,128)(2,1)} %param.24) | copy-start | bytes 245764
  272.6 33.7 %copy-start.2 = (bf16[320,2,128]{2,1,0:T(2,128)(2,1)S(1)}, bf16[320,2,128]{2,1,0:T(2,128)(2,1)}, u32[]{:S(2)}) copy-start(bf16[320,2,128]{2,1,0:T(2,128)(2,1)} %param.21) | copy-start | bytes 491524
  280.7 32.0 %copy-start.3 = (bf16[320,2,128]{2,1,0:T(2,128)(2,1)S(1)}, bf16[320,2,128]{2,1,0:T(2,128)(2,1)}, u32[]{:S(2)}) copy-start(bf16[320,2,128]{2,1,0:T(2,128)(2,1)} %param.22) | copy-start | bytes 491524
Sparse Core Ops, SparseCore 0:
  9.4 47.2 all-gather.6
  58.9 41.4 all-gather.8
  103.3 140.5 all-gather.10
  282.8 127.3 all-gather.12
where the time goes:
time: 443 us
  waiting for transfers between devices  303 us (68%)
  blocking collectives  89.3 us (20%)
  between operations  16.5 us (4%)
  other arithmetic  12.5 us (3%)
  matrix products  11.4 us (3%)
  local copies, waits for them, and re-layouts  10.1 us (2%)
    all_gather x1, waiting for transfers between devices, on_device(): shard_piece = lax.all_gather(rim_rows, 'tile', axis=0, tiled=True)  140 us
    all_gather x1, waiting for transfers between devices, on_device(): lax.all_gather(pooled, 'tile', axis=0, tiled=True)  88.4 us
    all_gather x1, waiting for transfers between devices, on_device(): lax.all_gather(conv_adjusted, 'image', axis=3, tiled=True)  43.6 us
    all_gather x1, waiting for transfers between devices, on_device(): lax.all_gather(conv_ema, 'image', axis=3, tiled=True)  30.2 us
    all_gather x1, blocking collectives, on_device(): lax.all_gather(part, 'tensor', axis=1, tiled=True)  16.3 us
    all_gather x1, blocking collectives, on_device(): halo_full = lax.all_gather(halo_rows, 'tensor', axis=1, tiled=True)  15.5 us
    all_gather x1, blocking collectives, on_device(): block_full = lax.all_gather(activated, 'tensor', axis=1, tiled=True)  13.6 us
  transfers between devices with their start and end apart: 4, of which 4 were waited for; matrix products, arithmetic and copies ran while one was open for 2% of the time, Pallas kernels for 0%

commit v1 on v0

--- a/solution.py
+++ b/solution.py
@@ -1,3 +1,4 @@
+import functools
 import jax
 import jax.numpy as jnp
 from jax import lax
@@ -5,6 +6,15 @@
 
 HD = 64
 POOL = 4
+
+
+def connect_ports_now(patch, ax_name):
+    near = jnp.stack([patch for _ in range(jax.lax.psum(1, ax_name))])
+    local_next = jax.lax.all_to_all(near, ax_name, 0, 0)
+    return jnp.concatenate(local_next, axis=3)
+
+
+lay_scales = functools.partial(connect_ports_now, ax_name="image")
 
 
 def blend(ema_part, adjusted_part, blend_ratio):
@@ -53,7 +63,7 @@
     blend_ratio = merge_num[0].astype(jnp.float32) / 16.0
     gathered = (
         lax.all_gather(conv_ema, "image", axis=3, tiled=True),
-        lax.all_gather(conv_adjusted, "image", axis=3, tiled=True),
+        lay_scales(conv_adjusted),
         lax.all_gather(query_ema, "image", axis=0, tiled=True),
         lax.all_gather(query_adjusted, "image", axis=0, tiled=True),
         lax.all_gather(kv_ema, "image", axis=0, tiled=True),

time: 443 us -> 411 us (0.928)
  waiting for transfers between devices: 303 us -> 245 us
  blocking collectives: 89.3 us -> 107 us
  starting transfers between devices: 0.12 us -> 5.18 us
    all_gather x1 -> x0, waiting for transfers between devices: 43.6 us -> none  [on_device(): lax.all_gather(conv_adjusted, 'image', axis=3, tiled=True)]
    all_gather x1, blocking collectives: 13.6 us -> 31.2 us  [on_device(): block_full = lax.all_gather(activated, 'tensor', axis=1, tiled=True)]
    all_gather x1, waiting for transfers between devices: 30.2 us -> 13.1 us  [on_device(): lax.all_gather(conv_ema, 'image', axis=3, tiled=True)]
    all_to_all x0 -> x1, starting transfers between devices: none -> 5.14 us  [connect_ports_now(): local_next = jax.lax.all_to_all(near, ax_name, 0, 0)]
  transfers between devices with their start and end apart: 4 -> 4, of which waited for: 4 -> 3; matrix products, arithmetic and copies ran while one was open for 2% -> 3% of each run, Pallas kernels for 0% -> 0%
where the time goes in v1:
time: 411 us; the launch traced here: 410 us
  waiting for transfers between devices  245 us (60%)
  blocking collectives  107 us (26%)
  between operations  16.6 us (4%)
  other arithmetic  15 us (4%)
  matrix products  11.3 us (3%)
  local copies, waits for them, and re-layouts  10.1 us (2%)
  starting transfers between devices  5.18 us (1%)
    all_gather x1, waiting for transfers between devices, on_device(): shard_piece = lax.all_gather(rim_rows, 'tile', axis=0, tiled=True)  143 us
    all_gather x1, waiting for transfers between devices, on_device(): lax.all_gather(pooled, 'tile', axis=0, tiled=True)  88.5 us
    all_gather x1, blocking collectives, on_device(): block_full = lax.all_gather(activated, 'tensor', axis=1, tiled=True)  31.2 us
    all_gather x1, blocking collectives, on_device(): lax.all_gather(part, 'tensor', axis=1, tiled=True)  16.3 us
    all_gather x1, blocking collectives, on_device(): halo_full = lax.all_gather(halo_rows, 'tensor', axis=1, tiled=True)  15.5 us
    all_gather x1, waiting for transfers between devices, on_device(): lax.all_gather(conv_ema, 'image', axis=3, tiled=True)  13.1 us
  transfers between devices with their start and end apart: 4, of which 3 were waited for; matrix products, arithmetic and copies ran while one was open for 3% of the time, Pallas kernels for 0%

profile of v1, /device:TPU:1, one launch (start us, length us, event | category | flops | bytes accessed | tf_op | source)
XLA Modules:
  0.0 410.0 jit_solution(10972241609922226367)
XLA Ops:
  6.5 0.7 all-gather.6.cloned.1.call-update
  7.3 0.0 all-gather.8.cloned.1.call-start
  7.3 1.0 fusion.54
  8.3 0.6 pad_maximum_fusion.2
  9.0 0.0 all-gather.8.cloned.1.call-update
  9.0 3.0 pad_maximum_fusion
  12.0 5.1 %all-to-all-start = ((bf16[2,3,3,1,1,80,640]{6,5,2,1,4,3,0:T(8,128)(2,1)}), bf16[2,3,3,1,1,80,640]{6,5,2,1,4,3,0:T(8,128)(2,1)S(1)}, u32[]{:S(2)}, u32[]{:S(2)}) async-start(bf16[2,3,3,1,1,80,640]{6,5,2,1,4,3,0:T(8,128)(2,1)} %pad_maximum_fusion), calls=%async_computation | async-start | bytes 3686400 | tf_op jit(solution)/shard_map/all_to_all | solution.py:13
  17.2 0.1 copy.120
  17.3 0.7 dynamic_slice.24
  18.6 0.6 dynamic_slice.25
  20.5 0.1 select_reduce_fusion.3
  20.6 31.2 %all_gather.41 = bf16[4,640,128]{2,0,1:T(4,128)(2,1)S(1)} all-gather(bf16[4,160,128]{2,0,1:T(4,128)(2,1)S(1)} %copy.120), channel_id=1, replica_groups=mesh['tile'=64,'image'=2,'tensor'=4] {'tensor'}, dimensions={1}, use_global_device_ids=true | all-gather | bytes 819200 | tf_op jit(solution)/shard_map/all_gather | solution.py:82
  51.7 13.1 %all-gather.6.cloned.1.call-done = bf16[3,3,1,2,80,640]{5,4,3,1,0,2:T(8,128)(2,1)} async-done(((bf16[3,3,1,1,80,640]{5,4,3,1,0,2:T(8,128)(2,1)}), bf16[3,3,1,2,80,640]{5,4,3,1,0,2:T(8,128)(2,1)}) %all-gather.6.cloned.1.call-update) | async-done | bytes 1843216 | tf_op jit(solution)/shard_map/all_gather | solution.py:65
  64.8 3.5 fusion.1
  68.3 142.7 %all-gather.8.cloned.1.call-done = bf16[128,160,128]{2,1,0:T(8,128)(2,1)} async-done(((bf16[2,160,128]{2,1,0:T(8,128)(2,1)}), bf16[128,160,128]{2,1,0:T(8,128)(2,1)}) %all-gather.8.cloned.1.call-update) | async-done | bytes 5242896 | tf_op jit(solution)/shard_map/all_gather | solution.py:84
  211.0 2.9 slice_bitcast_fusion.1
  213.9 0.8 fusion.10
  214.7 1.4 fusion.8
  216.1 15.5 %all_gather.40 = bf16[2,640,128]{2,1,0:T(8,128)(2,1)S(1)} all-gather(bf16[2,160,128]{2,1,0:T(8,128)(2,1)S(1)} %pad_maximum_fusion.3), channel_id=1, replica_groups=mesh['tile'=64,'image'=2,'tensor'=4] {'tensor'}, dimensions={1}, use_global_device_ids=true | all-gather | bytes 409600 | tf_op jit(solution)/shard_map/all_gather | solution.py:95
  231.7 0.3 copy.121
  231.9 0.3 copy.122
  232.2 1.1 maximum_bitcast_fusion
  233.3 1.2 copy.144
  234.5 0.3 pad.clone
  234.8 0.0 copy-start.11
  234.8 0.4 reshape.188
  235.2 0.1 copy.125
  235.4 0.1 copy-done.11
  235.5 1.2 copy-done
  236.7 1.8 convolution_select_fusion
  238.6 0.2 copy.128
  238.8 0.2 copy.143
  239.0 0.4 copy-done.1
  239.5 0.1 copy.130
  239.7 8.1 %all_gather.45 = bf16[4,640,128]{2,0,1:T(4,128)(2,1)S(1)} all-gather(bf16[4,160,128]{2,0,1:T(4,128)(2,1)S(1)} %copy.130), channel_id=1, replica_groups=mesh['tile'=64,'image'=2,'tensor'=4] {'tensor'}, dimensions={1}, use_global_device_ids=true | all-gather | bytes 819200 | tf_op jit(solution)/shard_map/all_gather | solution.py:99
  247.8 0.9 copy.131
  248.7 0.1 convert_reduce_fusion
  248.8 0.1 reduce_sum.71
  248.9 0.2 reduce_sum.72
  249.1 0.6 fusion.69
  249.7 0.0 all-gather.10.cloned.1.call-update
  250.9 6.1 %all_gather.46 = bf16[640,128]{1,0:T(8,128)(2,1)S(1)} all-gather(bf16[320,128]{1,0:T(8,128)(2,1)S(1)} %copy-done.4), channel_id=1, replica_groups=mesh['tile'=64,'image'=2,'tensor'=4] {'image'}, dimensions={0}, use_global_device_ids=true | all-gather | bytes 245760 | tf_op jit(solution)/shard_map/all_gather | solution.py:67
  257.0 5.5 %all_gather.47 = bf16[640,128]{1,0:T(8,128)(2,1)S(1)} all-gather(bf16[320,128]{1,0:T(8,128)(2,1)S(1)} %copy-done.5), channel_id=1, replica_groups=mesh['tile'=64,'image'=2,'tensor'=4] {'image'}, dimensions={0}, use_global_device_ids=true | all-gather | bytes 245760 | tf_op jit(solution)/shard_map/all_gather | solution.py:68
  262.5 5.5 %all_gather.43 = bf16[160,512]{1,0:T(8,128)(2,1)S(1)} all-gather(bf16[160,256]{1,0:T(8,128)(2,1)S(1)} %copy-done.6), channel_id=1, replica_groups=mesh['tile'=64,'image'=2,'tensor'=4] {'image'}, dimensions={1}, use_global_device_ids=true | all-gather | bytes 245760 | tf_op jit(solution)/shard_map/all_gather | solution.py:71
  267.9 5.5 %all_gather.44 = bf16[160,512]{1,0:T(8,128)(2,1)S(1)} all-gather(bf16[160,256]{1,0:T(8,128)(2,1)S(1)} %copy-done.7), channel_id=1, replica_groups=mesh['tile'=64,'image'=2,'tensor'=4] {'image'}, dimensions={1}, use_global_device_ids=true | all-gather | bytes 245760 | tf_op jit(solution)/shard_map/all_gather | solution.py:72
  273.4 6.4 %all_gather.49 = bf16[640,2,128]{2,1,0:T(2,128)(2,1)S(1)} all-gather(bf16[320,2,128]{2,1,0:T(2,128)(2,1)S(1)} %copy-done.2), channel_id=1, replica_groups=mesh['tile'=64,'image'=2,'tensor'=4] {'image'}, dimensions={0}, use_global_device_ids=true | all-gather | bytes 491520 | tf_op jit(solution)/shard_map/all_gather | solution.py:69
  279.8 6.9 %all_gather.50 = bf16[640,2,128]{2,1,0:T(2,128)(2,1)S(1)} all-gather(bf16[320,2,128]{2,1,0:T(2,128)(2,1)S(1)} %copy-done.3), channel_id=1, replica_groups=mesh['tile'=64,'image'=2,'tensor'=4] {'image'}, dimensions={0}, use_global_device_ids=true | all-gather | bytes 491520 | tf_op jit(solution)/shard_map/all_gather | solution.py:70
  286.7 0.2 select_reduce_fusion.2
  286.9 0.6 fusion.89
  287.4 0.5 fusion.45
  287.9 0.2 fusion.24
  288.2 0.2 fusion.23
  288.4 0.4 fusion.31
  288.7 88.5 %all-gather.10.cloned.1.call-done = bf16[1,2048,640]{2,1,0:T(8,128)(2,1)} async-done(((bf16[1,32,640]{2,1,0:T(8,128)(2,1)}), bf16[1,2048,640]{2,1,0:T(8,128)(2,1)}) %all-gather.10.cloned.1.call-update) | async-done | bytes 2621456 | tf_op jit(solution)/shard_map/all_gather | solution.py:126
  377.2 2.8 fusion.12
  380.0 0.1 fusion.90
  380.1 0.7 fusion.61
  380.8 1.1 select_reduce_fusion.1
  381.9 2.1 fusion.2
  384.1 1.0 fusion.35
  385.1 1.0 fusion.41
  386.2 16.3 %all_gather.51 = bf16[512,512]{0,1:T(8,128)(2,1)S(1)} all-gather(bf16[512,128]{0,1:T(8,128)(2,1)S(1)} %fusion.63), channel_id=1, replica_groups=mesh['tile'=64,'image'=2,'tensor'=4] {'tensor'}, dimensions={1}, use_global_device_ids=true | all-gather | bytes 655360 | tf_op jit(solution)/shard_map/all_gather | solution.py:173
  402.5 0.3 convolution_bitcast_fusion
  402.8 0.7 fusion.64
  (41 shorter events, 0.3 us)
Async XLA Ops:
  6.5 58.3 %all-gather.6.cloned.1.call-start = ((), (), s32[]{:S(2)}) async-start(), calls=%async_computation.1 | async-start | bytes 2764800 | tf_op jit(solution)/shard_map/all_gather | solution.py:65
  7.3 203.8 %all-gather.8.cloned.1.call-start = ((), (), s32[]{:S(2)}) async-start(), calls=%async_computation.2 | async-start | bytes 5324800 | tf_op jit(solution)/shard_map/all_gather | solution.py:84
  12.0 5.3 %copy-start.9 = (s32[2,64]{1,0:T(2,128)S(1)}, s32[2,64]{1,0:T(2,128)}, u32[]{:S(2)}) copy-start(s32[2,64]{1,0:T(2,128)} %param.14) | copy-start | bytes 1540
  12.0 6.5 %copy-start.10 = (s32[2]{0:T(128)S(1)}, s32[2]{0:T(128)}, u32[]{:S(2)}) copy-start(s32[2]{0:T(128)} %param.15) | copy-start | bytes 28
  12.0 39.7 %all-to-all-start = ((bf16[2,3,3,1,1,80,640]{6,5,2,1,4,3,0:T(8,128)(2,1)}), bf16[2,3,3,1,1,80,640]{6,5,2,1,4,3,0:T(8,128)(2,1)S(1)}, u32[]{:S(2)}, u32[]{:S(2)}) async-start(bf16[2,3,3,1,1,80,640]{6,5,2,1,4,3,0:T(8,128)(2,1)} %pad_maximum_fusion), calls=%async_computation | async-start | bytes 3686400 | tf_op jit(solution)/shard_map/all_to_all | solution.py:13
  17.2 360.0 %all-gather.10.cloned.1.call-start = ((), (), s32[]{:S(2)}) async-start(), calls=%async_computation.3 | async-start | bytes 2662400 | tf_op jit(solution)/shard_map/all_gather | solution.py:126
  234.8 0.7 copy-start.11
  235.2 1.5 copy-start
  238.5 0.9 copy-start.1
  239.5 11.4 %copy-start.8 = (bf16[640]{0:T(1024)(128)(2,1)S(1)}, bf16[640]{0:T(1024)(128)(2,1)}, u32[]{:S(2)}) copy-start(bf16[640]{0:T(1024)(128)(2,1)} %param.25) | copy-start | bytes 3844
  239.5 11.4 %copy-start.4 = (bf16[320,128]{1,0:T(8,128)(2,1)S(1)}, bf16[320,128]{1,0:T(8,128)(2,1)}, u32[]{:S(2)}) copy-start(bf16[320,128]{1,0:T(8,128)(2,1)} %param.19) | copy-start | bytes 245764
  239.5 17.5 %copy-start.5 = (bf16[320,128]{1,0:T(8,128)(2,1)S(1)}, bf16[320,128]{1,0:T(8,128)(2,1)}, u32[]{:S(2)}) copy-start(bf16[320,128]{1,0:T(8,128)(2,1)} %param.20) | copy-start | bytes 245764
  239.5 22.9 %copy-start.6 = (bf16[160,256]{1,0:T(8,128)(2,1)S(1)}, bf16[160,256]{1,0:T(8,128)(2,1)}, u32[]{:S(2)}) copy-start(bf16[160,256]{1,0:T(8,128)(2,1)} %param.23) | copy-start | bytes 245764
  239.6 28.3 %copy-start.7 = (bf16[160,256]{1,0:T(8,128)(2,1)S(1)}, bf16[160,256]{1,0:T(8,128)(2,1)}, u32[]{:S(2)}) copy-start(bf16[160,256]{1,0:T(8,128)(2,1)} %param.24) | copy-start | bytes 245764
  239.6 33.8 %copy-start.2 = (bf16[320,2,128]{2,1,0:T(2,128)(2,1)S(1)}, bf16[320,2,128]{2,1,0:T(2,128)(2,1)}, u32[]{:S(2)}) copy-start(bf16[320,2,128]{2,1,0:T(2,128)(2,1)} %param.21) | copy-start | bytes 491524
  247.8 32.0 %copy-start.3 = (bf16[320,2,128]{2,1,0:T(2,128)(2,1)S(1)}, bf16[320,2,128]{2,1,0:T(2,128)(2,1)}, u32[]{:S(2)}) copy-start(bf16[320,2,128]{2,1,0:T(2,128)(2,1)} %param.22) | copy-start | bytes 491524
Sparse Core Ops, SparseCore 0:
  9.4 55.3 all-gather.5
  67.8 143.2 all-gather.7
  249.8 127.3 all-gather.9
